TPU v7x, 32 devices: a whole 2x2x4 slice. The times are simulated.
32 devices in a mesh: grp: 4 (over y, core), shard: 8 (over z, x).
Axes of the slice: x: 2, y: 2, z: 4, core: 2. Of those that a mesh axis runs over, the one named last changes fastest.
Arguments:
- query_rows: bfloat16 [16, 6144], P('grp'), may hold values from -10 to 10
- key_cache: bfloat16 [16, 2048, 1024], P('grp', 'shard'), may hold values from -10 to 10
- value_cache: bfloat16 [16, 2048, 1024], P('grp', 'shard'), may hold values from -6 to 6
- lengths: int32 [16], P('grp'), may hold values from 2 to 2048
- attn_gain: float32 [6144], replicated, may hold values from 0.5 to 1.5
- router: bfloat16 [6144, 4], replicated, may hold values from -0.078125 to 0.078125
- expert_ids: int32 [16, 2], replicated, may hold values from 0 to 3, all different within a row; in each aligned block of 4 rows (0 to 3, 4 to 7, ...) at most 2 rows name the same one
- w_gate: bfloat16 [4, 6144, 8192], P('grp', None, 'shard'), may hold values from -0.078125 to 0.078125
- w_up: bfloat16 [4, 6144, 8192], P('grp', None, 'shard'), may hold values from -0.078125 to 0.078125
- w_down: bfloat16 [4, 8192, 6144], P('grp', 'shard'), may hold values from -0.0625 to 0.0625
Outputs:
- normed: bfloat16 [16, 6144], P('grp')
- expert_out: bfloat16 [16, 6144], P('grp', 'shard')
Inputs may be any that keep to these rules, and one draw needn't show every extreme that they name: `expert_ids`: the two ids of a row differ. Among the 4 rows of one index of grp (aligned blocks), no expert is named by more than 2 rows, a bound that some block reaches.
All inputs are finite; a program needn't handle non-finite values.
Results may differ from a plain program's by a relative error of at most 0.0095.
Values may be sent and summed in bfloat16 or wider, within the bound.
No kernel may reach another device: no remote copies, remote signals or barrier semaphores. Data moves between devices by JAX's collectives and lax.ppermute only.
A program may use at most 128 MiB of HBM per device.

v0:
```python
import math
import jax
import jax.numpy as jnp
from jax import lax
from jax.sharding import PartitionSpec as P

HEADS = 48
KV_HEADS = 8
HEAD_DIM = 128
BLOCK = 256
NEG_FILL = -1e30
CAP = 2


def slot_match(expert_ids, experts, rows_here, n_groups):
    ids = expert_ids.reshape(n_groups, rows_here, expert_ids.shape[1])
    hit = jnp.any(ids[None, :, :, :] == experts[:, None, None, None], axis=-1)
    rank = jnp.cumsum(hit.astype(jnp.int32), axis=-1) - 1
    slot = jnp.arange(CAP, dtype=jnp.int32)
    return hit[:, :, None, :] & (rank[:, :, None, :] == slot[None, None, :, None])


def shards(
    query_rows, key_cache, value_cache, lengths, attn_gain, router, expert_ids, w_gate, w_up, w_down
):
    rows_here = query_rows.shape[0]
    span = key_cache.shape[1]
    kv_share = HEADS // KV_HEADS
    n_grp = lax.axis_size("grp")
    n_shard = lax.axis_size("shard")
    grp_id = lax.axis_index("grp")
    shard_id = lax.axis_index("shard")
    n_blocks = span // BLOCK
    query_heads = query_rows.reshape(rows_here, KV_HEADS, kv_share, HEAD_DIM)
    key_heads = key_cache.reshape(rows_here, span, KV_HEADS, HEAD_DIM)
    value_heads = value_cache.reshape(rows_here, n_blocks, BLOCK, KV_HEADS, HEAD_DIM)
    scores = jnp.einsum(
        "rgjd,rtgd->rgjt", query_heads, key_heads, preferred_element_type=jnp.float32
    ) / math.sqrt(HEAD_DIM)
    position = shard_id * span + jnp.arange(span, dtype=jnp.int32)
    live_mask = (position[None, :] < lengths[:, None])[:, None, None, :]
    scores = jnp.where(live_mask, scores, NEG_FILL)
    scores = scores.reshape(rows_here, KV_HEADS, kv_share, n_blocks, BLOCK)
    live_blocks = live_mask.reshape(rows_here, 1, 1, n_blocks, BLOCK)
    block_max = jnp.max(scores, axis=-1)
    block_probs = jnp.where(live_blocks, jnp.exp(scores - block_max[..., None]), 0.0).astype(
        jnp.bfloat16
    )
    block_sum = jnp.sum(block_probs.astype(jnp.float32), axis=-1)
    block_mix = jnp.einsum(
        "rgjbt,rbtgd->rgjbd", block_probs, value_heads, preferred_element_type=jnp.float32
    )
    dev_max = jnp.max(block_max, axis=-1)
    dev_factor = jnp.exp(block_max - dev_max[..., None])
    dev_sum = jnp.sum(block_sum * dev_factor, axis=-1).reshape(rows_here, HEADS)
    dev_mix = jnp.sum(block_mix * dev_factor[..., None], axis=-2).reshape(
        rows_here, HEADS, HEAD_DIM
    )
    dev_max = dev_max.reshape(rows_here, HEADS)
    per_chunk = HEADS // n_shard
    mix_out = dev_mix.reshape(rows_here, n_shard, per_chunk, HEAD_DIM)
    side = jnp.concatenate(
        [
            dev_max.reshape(rows_here, n_shard, per_chunk),
            dev_sum.reshape(rows_here, n_shard, per_chunk),
        ],
        axis=-1,
    )
    side = jnp.pad(side, ((0, 0), (0, 0), (0, HEAD_DIM - 2 * per_chunk)))
    packed = jnp.concatenate([mix_out, side[:, :, None, :]], axis=2)
    packed = jnp.transpose(packed, (1, 0, 2, 3))
    stats = lax.all_to_all(packed, "shard", 0, 0, tiled=True)
    got_mix = stats[:, :, :per_chunk, :]
    got_max = stats[:, :, per_chunk, :per_chunk]
    got_sum = stats[:, :, per_chunk, per_chunk : 2 * per_chunk]
    top = jnp.max(got_max, axis=0)
    factor = jnp.exp(got_max - top[None])
    whole_sum = jnp.sum(got_sum * factor, axis=0)
    whole_mix = jnp.sum(got_mix * factor[..., None], axis=0)
    chunk = (whole_mix / whole_sum[..., None]).reshape(rows_here, per_chunk * HEAD_DIM)
    n_dev = n_grp * n_shard
    spread = jnp.broadcast_to(chunk.astype(jnp.bfloat16)[None], (n_dev,) + chunk.shape)
    gathered = lax.all_to_all(spread, ("grp", "shard"), 0, 0, tiled=True).astype(jnp.float32)
    gathered = gathered.reshape(n_grp, n_shard, rows_here, per_chunk * HEAD_DIM)
    attended = jnp.transpose(gathered, (0, 2, 1, 3)).reshape(n_grp * rows_here, -1)
    mean_square = jnp.mean(attended * attended, axis=-1, keepdims=True)
    normed_all = (attended * lax.rsqrt(mean_square + 1e-05) * attn_gain).astype(jnp.bfloat16)
    normed = lax.dynamic_slice_in_dim(normed_all, grp_id * rows_here, rows_here, 0)
    logits = jnp.dot(normed_all, router, preferred_element_type=jnp.float32)
    experts = router.shape[1]
    expert_range = jnp.arange(experts, dtype=jnp.int32)
    expert_hit = expert_ids[:, :, None] == expert_range[None, None, :]
    chosen = jnp.sum(jnp.where(expert_hit, logits[:, None, :], 0.0), axis=-1)
    first_weight = jax.nn.sigmoid(chosen[:, 0] - chosen[:, 1])
    route_weight = jnp.stack([first_weight, 1.0 - first_weight], axis=1)
    local_experts = w_gate.shape[0]
    assert local_experts == 1
    width = normed_all.shape[1]
    total = jnp.zeros((n_grp * rows_here, width), jnp.float32)
    for local in range(local_experts):
        expert_index = grp_id * local_experts + local
        coefficient = jnp.sum(jnp.where(expert_ids == expert_index, route_weight, 0.0), axis=-1)
        gate_proj = jnp.dot(normed_all, w_gate[local], preferred_element_type=jnp.float32)
        up_proj = jnp.dot(normed_all, w_up[local], preferred_element_type=jnp.float32)
        hidden = (jax.nn.silu(gate_proj) * up_proj).astype(jnp.bfloat16)
        expert_y = jnp.dot(hidden, w_down[local], preferred_element_type=jnp.float32)
        total = total + coefficient[:, None] * expert_y
    out_width = width // n_shard
    sending = slot_match(expert_ids, (grp_id * local_experts)[None], rows_here, n_grp)[0]
    grouped = total.reshape(n_grp, 1, rows_here, width)
    picked = jnp.sum(jnp.where(sending[..., None], grouped, 0.0), axis=2)
    blocks = picked.reshape(n_grp, CAP, n_shard, out_width)
    blocks = jnp.transpose(blocks, (0, 2, 1, 3)).reshape(n_dev, CAP, out_width)
    arrived = lax.all_to_all(blocks.astype(jnp.bfloat16), ("grp", "shard"), 0, 0, tiled=True)
    arrived = arrived.astype(jnp.float32)
    per_expert = jnp.sum(arrived.reshape(n_grp, n_shard, CAP, out_width), axis=1)
    own_ids = lax.dynamic_slice_in_dim(expert_ids, grp_id * rows_here, rows_here, 0)
    homes = slot_match(own_ids, jnp.arange(n_grp, dtype=jnp.int32) * local_experts, rows_here, 1)[
        :, 0
    ]
    spread_back = jnp.where(homes[..., None], per_expert[:, :, None, :], 0.0)
    result = jnp.sum(spread_back, axis=(0, 1))
    return (normed, result.astype(jnp.bfloat16))


def solution(mesh):
    in_specs = (
        P("grp", None),
        P("grp", "shard", None),
        P("grp", "shard", None),
        P("grp"),
        P(),
        P(),
        P(),
        P("grp", None, "shard"),
        P("grp", None, "shard"),
        P("grp", "shard", None),
    )
    out_specs = (P("grp", None), P("grp", "shard"))
    return jax.shard_map(shards, mesh=mesh, in_specs=in_specs, out_specs=out_specs, check_vma=False)
```

profile of v0, /device:TPU:0, one launch (start us, length us, event | category | flops | bytes accessed | tf_op | source)
XLA Modules:
  0.0 63.7 jit_solution(13962101609671001244)
XLA Ops:
  0.7 1.0 %reshape.264 = bf16[4,8,6,128]{3,2,1,0:T(8,128)(2,1)S(1)} reshape(bf16[4,6144]{1,0:T(4,128)(2,1)} %param.10) | data formatting | bytes 98304 | tf_op jit(solution)/shard_map/reshape | solution.py:34
  1.7 0.9 %broadcast_compare_fusion = pred[4,256]{1,0:T(4,128)(4,1)S(1)} fusion(s32[256]{0:T(256)S(1)} %iota_add_fusion, s32[4]{0:T(128)} %param.13), kind=kLoop, calls=%fused_computation.57 | loop fusion | flops 1024 | bytes 2064 | tf_op jit(solution)/shard_map/lt | solution.py:41
  2.6 0.7 %fusion.56 = (f32[4,8,6]{2,1,0:T(8,128)S(1)}, f32[4,8,6,256]{3,2,1,0:T(8,128)S(1)}) fusion(bf16[4,8,6,128]{3,2,1,0:T(8,128)(2,1)S(1)} %reshape.264, pred[4,256]{1,0:T(4,128)(4,1)S(1)} %broadcast_compare_fusion, bf16[4,256,1024]{2,1,0:T(8,128)(2,1)S(1)} %copy-done), kind=kOutput, calls=%fused_computation.72 | convolution fusion | flops 12730176 | bytes 2344704 | tf_op jit(solution)/shard_map/rgjd,rtgd->rgjt/dot_general | solution.py:37
  3.3 0.2 convert_reduce_fusion
  3.6 0.4 fusion.27
  4.1 0.7 %copy.82 = f32[8,4,7,128]{3,1,2,0:T(4,128)} copy(f32[8,4,7,128]{3,2,0,1:T(8,128)S(1)} %maximum_bitcast_fusion) | data formatting | bytes 229376 | tf_op jit(solution)/shard_map/transpose | solution.py:71
  4.8 7.4 %all-to-all-start = ((f32[8,4,7,128]{3,1,2,0:T(4,128)}), f32[8,4,7,128]{3,1,2,0:T(4,128)S(1)}, u32[]{:S(2)}, u32[]{:S(2)}) async-start(f32[8,4,7,128]{3,1,2,0:T(4,128)} %copy.82), calls=%async_computation | async-start | bytes 229376 | tf_op jit(solution)/shard_map/all_to_all | solution.py:72
  12.4 0.2 reduce_window_sum.23
  12.6 0.2 reduce_window_sum.22
  12.8 6.6 %all-to-all-done = f32[8,4,7,128]{3,1,2,0:T(4,128)S(1)} async-done(((f32[8,4,7,128]{3,1,2,0:T(4,128)}), f32[8,4,7,128]{3,1,2,0:T(4,128)S(1)}, u32[]{:S(2)}, u32[]{:S(2)}) %all-to-all-start) | async-done | bytes 114720 | tf_op jit(solution)/shard_map/all_to_all | solution.py:72
  19.5 0.1 fusion.46
  19.6 0.1 copy.84
  19.7 0.1 copy.85
  19.8 0.1 fusion.38
  20.0 0.7 %broadcast_in_dim.116 = bf16[32,4,768]{2,1,0:T(4,128)(2,1)} broadcast(bf16[4,768]{1,0:T(4,128)(2,1)S(1)} %fusion.48), dimensions={1,2} | broadcast | bytes 202752 | tf_op jit(solution)/shard_map/broadcast_in_dim | solution.py:82
  20.7 2.6 %all-to-all-start.1 = ((bf16[32,4,768]{2,1,0:T(4,128)(2,1)}), bf16[32,4,768]{2,1,0:T(4,128)(2,1)S(1)}, u32[]{:S(2)}, u32[]{:S(2)}) async-start(bf16[32,4,768]{2,1,0:T(4,128)(2,1)} %broadcast_in_dim.116), calls=%async_computation.1 | async-start | bytes 393216 | tf_op jit(solution)/shard_map/all_to_all | solution.py:83
  23.3 8.5 %all-to-all-done.1 = bf16[32,4,768]{2,1,0:T(4,128)(2,1)S(1)} async-done(((bf16[32,4,768]{2,1,0:T(4,128)(2,1)}), bf16[32,4,768]{2,1,0:T(4,128)(2,1)S(1)}, u32[]{:S(2)}, u32[]{:S(2)}) %all-to-all-start.1) | async-done | bytes 196640 | tf_op jit(solution)/shard_map/all_to_all | solution.py:83
  31.9 0.1 copy.98
  32.1 0.1 multiply_reduce_fusion
  32.2 0.1 copy.88
  32.4 0.1 multiply_convert_fusion.1
  32.5 0.2 fusion.57
  32.7 0.1 multiply_convert_fusion
  33.0 6.3 %fusion.4 = f32[16,1024]{1,0:T(8,128)S(1)} fusion(bf16[16,6144]{1,0:T(8,128)(2,1)S(1)} %bitcast.104, bf16[1,6144,1024]{2,1,0:T(8,128)(2,1)} %param.17), kind=kOutput, calls=%fused_computation.4 | convolution fusion | flops 201326592 | bytes 12845056 | tf_op jit(solution)/shard_map/dot_general | solution.py:103
  39.3 11.5 %fusion.6 = f32[16,6144]{1,0:T(8,128)S(1)} fusion(bf16[1,1024,6144]{2,1,0:T(8,128)(2,1)} %param.19, bf16[16,6144]{1,0:T(8,128)(2,1)S(1)} %bitcast.105, bf16[1,6144,1024]{2,1,0:T(8,128)(2,1)} %param.18, f32[16]{0:T(128)S(1)} %fusion.50, f32[16,1024]{1,0:T(8,128)S(1)} %fusion.4), kind=kOutput, calls=%fused_computation.6 | convolution fusion | flops 402849792 | bytes 25821248 | tf_op jit(solution)/shard_map/dot_general | solution.py:106
  50.8 0.1 broadcast_in_dim.122
  50.9 0.6 select_reduce_fusion
  51.7 0.7 %copy.91 = bf16[32,2,768]{2,1,0:T(2,128)(2,1)} copy(bf16[32,2,768]{2,0,1:T(8,128)(2,1)S(1)} %bitcast.109) | data formatting | bytes 196608 | tf_op jit(solution)/shard_map/convert_element_type | solution.py:114
  52.4 2.9 %all-to-all-start.2 = ((bf16[32,2,768]{2,1,0:T(2,128)(2,1)}), bf16[32,2,768]{2,1,0:T(2,128)(2,1)S(1)}, u32[]{:S(2)}, u32[]{:S(2)}) async-start(bf16[32,2,768]{2,1,0:T(2,128)(2,1)} %copy.91), calls=%async_computation.2 | async-start | bytes 196608 | tf_op jit(solution)/shard_map/all_to_all | solution.py:114
  55.3 0.7 %constant_dynamic-slice_fusion.1 = bf16[4,6144]{1,0:T(4,128)(2,1)} fusion(bf16[16,6144]{1,0:T(8,128)(2,1)S(1)} %multiply_convert_fusion.1, s32[]{:T(128)S(6)} %select_n.31), kind=kLoop, calls=%fused_computation.66 | loop fusion | bytes 98308 | tf_op jit(solution)/shard_map/dynamic_slice | solution.py:88
  56.0 6.9 %all-to-all-done.2 = bf16[32,2,768]{2,1,0:T(2,128)(2,1)S(1)} async-done(((bf16[32,2,768]{2,1,0:T(2,128)(2,1)}), bf16[32,2,768]{2,1,0:T(2,128)(2,1)S(1)}, u32[]{:S(2)}, u32[]{:S(2)}) %all-to-all-start.2) | async-done | bytes 98336 | tf_op jit(solution)/shard_map/all_to_all | solution.py:114
  63.0 0.7 %select_reduce_fusion.1 = bf16[4,768]{1,0:T(4,128)(2,1)} fusion(f32[4,2,768]{2,1,0:T(2,128)S(1)} %convert_reduce_fusion.1, pred[4,2,4]{2,1,0:T(4,128)(4,1)S(1)} %compare_and_fusion.1), kind=kLoop, calls=%fused_computation.32 | loop fusion | flops 46080 | bytes 30752 | tf_op jit(solution)/shard_map/reduce_sum | solution.py:122
  (39 shorter events, 0.9 us)
Async XLA Ops:
  0.6 1.9 %copy-start = (bf16[4,256,1024]{2,1,0:T(8,128)(2,1)S(1)}, bf16[4,256,1024]{2,1,0:T(8,128)(2,1)}, u32[]{:S(2)}) copy-start(bf16[4,256,1024]{2,1,0:T(8,128)(2,1)} %param.11) | copy-start | bytes 6291460
  1.7 1.9 %copy-start.1 = (bf16[4,256,1024]{2,1,0:T(8,128)(2,1)S(1)}, bf16[4,256,1024]{2,1,0:T(8,128)(2,1)}, u32[]{:S(2)}) copy-start(bf16[4,256,1024]{2,1,0:T(8,128)(2,1)} %param.12) | copy-start | bytes 6291460
  3.3 8.9 %copy-start.2 = (f32[6144]{0:T(1024)S(1)}, f32[6144]{0:T(1024)}, u32[]{:S(2)}) copy-start(f32[6144]{0:T(1024)} %param.14) | copy-start | bytes 73732
  3.3 8.9 %copy-start.3 = (s32[16,2]{0,1:T(2,128)S(1)}, s32[16,2]{0,1:T(2,128)}, u32[]{:S(2)}) copy-start(s32[16,2]{0,1:T(2,128)} %param.16) | copy-start | bytes 388
  4.8 27.7 %copy-start.4 = (bf16[6144,4]{0,1:T(4,128)(2,1)S(1)}, bf16[6144,4]{0,1:T(4,128)(2,1)}, u32[]{:S(2)}) copy-start(bf16[6144,4]{0,1:T(4,128)(2,1)} %param.15) | copy-start | bytes 147460
  4.8 14.6 %all-to-all-start = ((f32[8,4,7,128]{3,1,2,0:T(4,128)}), f32[8,4,7,128]{3,1,2,0:T(4,128)S(1)}, u32[]{:S(2)}, u32[]{:S(2)}) async-start(f32[8,4,7,128]{3,1,2,0:T(4,128)} %copy.82), calls=%async_computation | async-start | bytes 229376 | tf_op jit(solution)/shard_map/all_to_all | solution.py:72
  20.7 11.1 %all-to-all-start.1 = ((bf16[32,4,768]{2,1,0:T(4,128)(2,1)}), bf16[32,4,768]{2,1,0:T(4,128)(2,1)S(1)}, u32[]{:S(2)}, u32[]{:S(2)}) async-start(bf16[32,4,768]{2,1,0:T(4,128)(2,1)} %broadcast_in_dim.116), calls=%async_computation.1 | async-start | bytes 393216 | tf_op jit(solution)/shard_map/all_to_all | solution.py:83
  52.4 10.5 %all-to-all-start.2 = ((bf16[32,2,768]{2,1,0:T(2,128)(2,1)}), bf16[32,2,768]{2,1,0:T(2,128)(2,1)S(1)}, u32[]{:S(2)}, u32[]{:S(2)}) async-start(bf16[32,2,768]{2,1,0:T(2,128)(2,1)} %copy.91), calls=%async_computation.2 | async-start | bytes 196608 | tf_op jit(solution)/shard_map/all_to_all | solution.py:114
where the time goes:
time: 64.1 us; the launch traced here: 63.7 us
  waiting for transfers between devices  22 us (34%)
  matrix products  19.2 us (30%)
  starting transfers between devices  12.9 us (20%)
  local copies, waits for them, and re-layouts  4.82 us (8%)
  other arithmetic  3.87 us (6%)
  between operations  0.87 us (1%)
    dot_general x1, matrix products, shards(): jnp.dot(hidden, w_down[local], preferred_element_type=jnp.float32)  11.5 us
    all_to_all x1, waiting for transfers between devices, shards(): lax.all_to_all(spread, ('grp', 'shard'), 0, 0, tiled=True)  8.52 us
    all_to_all x1, starting transfers between devices, shards(): stats = lax.all_to_all(packed, 'shard', 0, 0, tiled=True)  7.38 us
    all_to_all x1, waiting for transfers between devices, shards(): lax.all_to_all(blocks.astype(jnp.bfloat16), ('grp', 'shard'), 0, 0, tiled...  6.9 us
    all_to_all x1, waiting for transfers between devices, shards(): stats = lax.all_to_all(packed, 'shard', 0, 0, tiled=True)  6.61 us
    dot_general x1, matrix products, shards(): jnp.dot(normed_all, w_gate[local], preferred_element_type=jnp.float32)  6.3 us
    all_to_all x1, starting transfers between devices, shards(): lax.all_to_all(blocks.astype(jnp.bfloat16), ('grp', 'shard'), 0, 0, tiled...  2.95 us
    all_to_all x1, starting transfers between devices, shards(): lax.all_to_all(spread, ('grp', 'shard'), 0, 0, tiled=True)  2.58 us
  transfers between devices with their start and end apart: 3, of which 3 were waited for; matrix products, arithmetic and copies ran while one was open for 2% of the time, Pallas kernels for 0%

commit v1 on v0

--- a/solution.py
+++ b/solution.py
@@ -10,6 +10,19 @@
 BLOCK = 256
 NEG_FILL = -1e30
 CAP = 2
+
+
+def balance_the_area(xx, d0, my_tile):
+    aux, r2 = (xx.shape[:d0], xx.shape[d0 + 1 :])
+    s_next = jnp.moveaxis(xx.reshape(*aux, my_tile, -1, *r2), d0, 0)
+    return s_next
+
+
+def state_chains(q_in, row_dim):
+    tall = list(q_in.shape[1:])
+    tall[row_dim] *= q_in.shape[0]
+    e_next = jnp.moveaxis(q_in, 0, row_dim).reshape(tall)
+    return e_next
 
 
 def slot_match(expert_ids, experts, rows_here, n_groups):
@@ -69,7 +82,16 @@
     side = jnp.pad(side, ((0, 0), (0, 0), (0, HEAD_DIM - 2 * per_chunk)))
     packed = jnp.concatenate([mix_out, side[:, :, None, :]], axis=2)
     packed = jnp.transpose(packed, (1, 0, 2, 3))
-    stats = lax.all_to_all(packed, "shard", 0, 0, tiled=True)
+    extra, z1 = (lax.psum(1, "shard"), lax.axis_index("shard"))
+    prior = balance_the_area(packed, 0, extra)
+    xs_all = [prior[z1]]
+    k0 = 1
+    while k0 < extra:
+        now = prior[z1 ^ k0]
+        xs_all.append(lax.ppermute(now, "shard", [(j, j ^ k0) for j in range(extra)]))
+        k0 += 1
+    prior = jnp.stack(xs_all)[z1 ^ jnp.arange(extra)]
+    stats = state_chains(prior, 0)
     got_mix = stats[:, :, :per_chunk, :]
     got_max = stats[:, :, per_chunk, :per_chunk]
     got_sum = stats[:, :, per_chunk, per_chunk : 2 * per_chunk]

time: 64.1 us -> 70.4 us (1.098)
  starting transfers between devices: 12.9 us -> 18.1 us
  matrix products: 19.2 us -> 20.8 us
    ppermute x0 -> x7, starting transfers between devices: none -> 12.6 us  [shards(): lax.ppermute(now, 'shard', [(j, j ^ k0) for j in range(extra)])]
    all_to_all x1 -> x0, starting transfers between devices: 7.38 us -> none  [shards(): stats = lax.all_to_all(packed, 'shard', 0, 0, tiled=True)]
    all_to_all x1 -> x0, waiting for transfers between devices: 6.61 us -> none  [shards(): stats = lax.all_to_all(packed, 'shard', 0, 0, tiled=True)]
    ppermute x0 -> x7, waiting for transfers between devices: none -> 6.31 us  [shards(): lax.ppermute(now, 'shard', [(j, j ^ k0) for j in range(extra)])]
    dot_general x1, matrix products: 0.43 us -> 2.01 us  [shards(): jnp.einsum('rgjbt,rbtgd->rgjbd', block_probs, value_heads, preferred_elem...]
    transpose x1 -> x0, local copies, waits for them, and re-layouts: 0.71 us -> none  [shards(): packed = jnp.transpose(packed, (1, 0, 2, 3))]
  transfers between devices with their start and end apart: 3 -> 9, of which waited for: 3 -> 4; matrix products, arithmetic and copies ran while one was open for 2% -> 2% of each run, Pallas kernels for 0% -> 0%
where the time goes in v1:
time: 70.4 us; the launch traced here: 70.1 us
  waiting for transfers between devices  21.7 us (31%)
  matrix products  20.8 us (30%)
  starting transfers between devices  18.1 us (26%)
  local copies, waits for them, and re-layouts  4.82 us (7%)
  other arithmetic  3.73 us (5%)
  between operations  0.99 us (1%)
    ppermute x7, starting transfers between devices, shards(): lax.ppermute(now, 'shard', [(j, j ^ k0) for j in range(extra)])  12.6 us
    dot_general x1, matrix products, shards(): jnp.dot(hidden, w_down[local], preferred_element_type=jnp.float32)  11.5 us
    all_to_all x1, waiting for transfers between devices, shards(): lax.all_to_all(spread, ('grp', 'shard'), 0, 0, tiled=True)  8.51 us
    all_to_all x1, waiting for transfers between devices, shards(): lax.all_to_all(blocks.astype(jnp.bfloat16), ('grp', 'shard'), 0, 0, tiled...  6.9 us
    dot_general x1, matrix products, shards(): jnp.dot(normed_all, w_gate[local], preferred_element_type=jnp.float32)  6.31 us
    ppermute x7, waiting for transfers between devices, shards(): lax.ppermute(now, 'shard', [(j, j ^ k0) for j in range(extra)])  6.31 us
    all_to_all x1, starting transfers between devices, shards(): lax.all_to_all(blocks.astype(jnp.bfloat16), ('grp', 'shard'), 0, 0, tiled...  2.95 us
    all_to_all x1, starting transfers between devices, shards(): lax.all_to_all(spread, ('grp', 'shard'), 0, 0, tiled=True)  2.58 us
  transfers between devices with their start and end apart: 9, of which 4 were waited for; matrix products, arithmetic and copies ran while one was open for 2% of the time, Pallas kernels for 0%

profile of v1, /device:TPU:0, one launch (start us, length us, event | category | flops | bytes accessed | tf_op | source)
XLA Modules:
  0.0 70.1 jit_solution(1269426190407753620)
XLA Ops:
  0.7 1.0 %reshape.308 = bf16[4,8,6,128]{3,2,1,0:T(8,128)(2,1)S(1)} reshape(bf16[4,6144]{1,0:T(4,128)(2,1)} %param.10) | data formatting | bytes 98304 | tf_op jit(solution)/shard_map/reshape | solution.py:47
  1.7 0.7 %broadcast_compare_fusion = pred[4,256]{1,0:T(4,128)(4,1)S(1)} fusion(s32[256]{0:T(256)S(1)} %iota_add_fusion, s32[4]{0:T(128)} %param.13), kind=kLoop, calls=%fused_computation.101 | loop fusion | flops 1024 | bytes 2064 | tf_op jit(solution)/shard_map/lt | solution.py:54
  2.4 0.7 %fusion.66 = (f32[4,8,6]{2,1,0:T(8,128)S(1)}, f32[4,8,6,256]{3,2,1,0:T(8,128)S(1)}) fusion(bf16[4,8,6,128]{3,2,1,0:T(8,128)(2,1)S(1)} %reshape.308, pred[4,256]{1,0:T(4,128)(4,1)S(1)} %broadcast_compare_fusion, bf16[4,256,1024]{2,1,0:T(8,128)(2,1)S(1)} %copy-done), kind=kOutput, calls=%fused_computation.115 | convolution fusion | flops 12730176 | bytes 2344704 | tf_op jit(solution)/shard_map/rgjd,rtgd->rgjt/dot_general | solution.py:50
  3.2 0.2 convert_reduce_fusion
  3.5 2.0 %fusion.27 = f32[4,8,6,128]{3,2,1,0:T(8,128)S(1)} fusion(f32[4,8,6]{2,1,0:T(8,128)S(1)} %get-tuple-element.15, f32[4,8,6,256]{3,2,1,0:T(8,128)S(1)} %get-tuple-element.17, f32[4,8,6]{2,1,0:T(8,128)S(1)} %get-tuple-element.16, pred[4,256]{1,0:T(4,128)(4,1)S(1)} %broadcast_compare_fusion, bf16[4,256,1024]{2,1,0:T(8,128)(2,1)} %param.12), kind=kOutput, calls=%fused_computation.18 | convolution fusion | flops 12754944 | bytes 2394624 | tf_op jit(solution)/shard_map/rgjbt,rbtgd->rgjbd/dot_general | solution.py:63
  5.6 3.0 %collective-permute-start = (f32[1,4,7,128]{3,1,2,0:T(4,128)S(1)}, f32[1,4,7,128]{3,1,2,0:T(4,128)S(1)}, u32[]{:S(2)}, u32[]{:S(2)}) collective-permute-start(f32[1,4,7,128]{3,1,2,0:T(4,128)S(1)} %bitcast.153), channel_id=1, source_target_pairs={{0,1},{1,0},{2,3},{3,2},{4,5},{5,4},{6,7},{7,6},{8,9},{9,8},{10,11... | collective-permute-start | bytes 43016 | tf_op jit(solution)/shard_map/ppermute | solution.py:91
  8.6 1.6 %collective-permute-start.1 = (f32[1,4,7,128]{3,1,2,0:T(4,128)S(1)}, f32[1,4,7,128]{3,1,2,0:T(4,128)S(1)}, u32[]{:S(2)}, u32[]{:S(2)}) collective-permute-start(f32[1,4,7,128]{3,1,2,0:T(4,128)S(1)} %bitcast.152), channel_id=1, source_target_pairs={{0,2},{1,3},{2,0},{3,1},{4,6},{5,7},{6,4},{7,5},{8,10},{9,11},{10,... | collective-permute-start | bytes 43016 | tf_op jit(solution)/shard_map/ppermute | solution.py:91
  10.2 3.0 %collective-permute-start.3 = (f32[1,4,7,128]{3,1,2,0:T(4,128)S(1)}, f32[1,4,7,128]{3,1,2,0:T(4,128)S(1)}, u32[]{:S(2)}, u32[]{:S(2)}) collective-permute-start(f32[1,4,7,128]{3,1,2,0:T(4,128)S(1)} %bitcast.150), channel_id=1, source_target_pairs={{0,4},{1,5},{2,6},{3,7},{4,0},{5,1},{6,2},{7,3},{8,12},{9,13},{10,... | collective-permute-start | bytes 43016 | tf_op jit(solution)/shard_map/ppermute | solution.py:91
  13.2 1.3 %collective-permute-start.4 = (f32[1,4,7,128]{3,1,2,0:T(4,128)S(1)}, f32[1,4,7,128]{3,1,2,0:T(4,128)S(1)}, u32[]{:S(2)}, u32[]{:S(2)}) collective-permute-start(f32[1,4,7,128]{3,1,2,0:T(4,128)S(1)} %bitcast.154), channel_id=1, source_target_pairs={{0,5},{1,4},{2,7},{3,6},{4,1},{5,0},{6,3},{7,2},{8,13},{9,12},{10,... | collective-permute-start | bytes 43016 | tf_op jit(solution)/shard_map/ppermute | solution.py:91
  14.7 0.2 reduce_window_sum.23
  15.0 0.2 reduce_window_sum.22
  15.2 3.6 %collective-permute-start.5 = (f32[1,4,7,128]{3,1,2,0:T(4,128)S(1)}, f32[1,4,7,128]{3,1,2,0:T(4,128)S(1)}, u32[]{:S(2)}, u32[]{:S(2)}) collective-permute-start(f32[1,4,7,128]{3,1,2,0:T(4,128)S(1)} %bitcast.156), channel_id=1, source_target_pairs={{0,6},{1,7},{2,4},{3,5},{4,2},{5,3},{6,0},{7,1},{8,14},{9,15},{10,... | collective-permute-start | bytes 43016 | tf_op jit(solution)/shard_map/ppermute | solution.py:91
  19.0 1.8 %collective-permute-done.5 = f32[1,4,7,128]{3,1,2,0:T(4,128)S(1)} collective-permute-done((f32[1,4,7,128]{3,1,2,0:T(4,128)S(1)}, f32[1,4,7,128]{3,1,2,0:T(4,128)S(1)}, u32[]{:S(2)}, u32[]{:S(2)}) %collective-permute-start.5) | collective-permute-done | bytes 14368 | tf_op jit(solution)/shard_map/ppermute | solution.py:91
  20.8 4.5 %collective-permute-done.6 = f32[1,4,7,128]{3,1,2,0:T(4,128)S(1)} collective-permute-done((f32[1,4,7,128]{3,1,2,0:T(4,128)S(1)}, f32[1,4,7,128]{3,1,2,0:T(4,128)S(1)}, u32[]{:S(2)}, u32[]{:S(2)}) %collective-permute-start.6) | collective-permute-done | bytes 14368 | tf_op jit(solution)/shard_map/ppermute | solution.py:91
  25.3 0.6 gather_fusion
  26.0 0.1 copy.104
  26.1 0.1 fusion.38
  26.4 0.7 %broadcast_in_dim.117 = bf16[32,4,768]{2,1,0:T(4,128)(2,1)} broadcast(bf16[4,768]{1,0:T(4,128)(2,1)S(1)} %fusion.57), dimensions={1,2} | broadcast | bytes 202752 | tf_op jit(solution)/shard_map/broadcast_in_dim | solution.py:104
  27.2 2.6 %all-to-all-start = ((bf16[32,4,768]{2,1,0:T(4,128)(2,1)}), bf16[32,4,768]{2,1,0:T(4,128)(2,1)S(1)}, u32[]{:S(2)}, u32[]{:S(2)}) async-start(bf16[32,4,768]{2,1,0:T(4,128)(2,1)} %broadcast_in_dim.117), calls=%async_computation | async-start | bytes 393216 | tf_op jit(solution)/shard_map/all_to_all | solution.py:105
  29.8 8.5 %all-to-all-done = bf16[32,4,768]{2,1,0:T(4,128)(2,1)S(1)} async-done(((bf16[32,4,768]{2,1,0:T(4,128)(2,1)}), bf16[32,4,768]{2,1,0:T(4,128)(2,1)S(1)}, u32[]{:S(2)}, u32[]{:S(2)}) %all-to-all-start) | async-done | bytes 196640 | tf_op jit(solution)/shard_map/all_to_all | solution.py:105
  38.4 0.1 copy.121
  38.5 0.1 multiply_reduce_fusion
  38.8 0.1 multiply_convert_fusion
  39.1 0.2 fusion.67
  39.4 6.3 %fusion.4 = f32[16,1024]{1,0:T(8,128)S(1)} fusion(bf16[16,6144]{1,0:T(8,128)(2,1)S(1)} %bitcast.141, bf16[1,6144,1024]{2,1,0:T(8,128)(2,1)} %param.17), kind=kOutput, calls=%fused_computation.5 | convolution fusion | flops 201326592 | bytes 12845056 | tf_op jit(solution)/shard_map/dot_general | solution.py:125
  45.7 11.5 %fusion.6 = f32[16,6144]{1,0:T(8,128)S(1)} fusion(bf16[1,1024,6144]{2,1,0:T(8,128)(2,1)} %param.19, bf16[16,6144]{1,0:T(8,128)(2,1)S(1)} %bitcast.142, bf16[1,6144,1024]{2,1,0:T(8,128)(2,1)} %param.18, f32[16]{0:T(128)S(1)} %fusion.59, f32[16,1024]{1,0:T(8,128)S(1)} %fusion.4), kind=kOutput, calls=%fused_computation.7 | convolution fusion | flops 402849792 | bytes 25821248 | tf_op jit(solution)/shard_map/dot_general | solution.py:128
  57.4 0.6 select_reduce_fusion
  58.1 0.7 %copy.112 = bf16[32,2,768]{2,1,0:T(2,128)(2,1)} copy(bf16[32,2,768]{2,0,1:T(8,128)(2,1)S(1)} %bitcast.146) | data formatting | bytes 196608 | tf_op jit(solution)/shard_map/convert_element_type | solution.py:136
  58.8 2.9 %all-to-all-start.1 = ((bf16[32,2,768]{2,1,0:T(2,128)(2,1)}), bf16[32,2,768]{2,1,0:T(2,128)(2,1)S(1)}, u32[]{:S(2)}, u32[]{:S(2)}) async-start(bf16[32,2,768]{2,1,0:T(2,128)(2,1)} %copy.112), calls=%async_computation.1 | async-start | bytes 196608 | tf_op jit(solution)/shard_map/all_to_all | solution.py:136
  61.8 0.7 constant_dynamic-slice_fusion.1
  62.4 6.9 %all-to-all-done.1 = bf16[32,2,768]{2,1,0:T(2,128)(2,1)S(1)} async-done(((bf16[32,2,768]{2,1,0:T(2,128)(2,1)}), bf16[32,2,768]{2,1,0:T(2,128)(2,1)S(1)}, u32[]{:S(2)}, u32[]{:S(2)}) %all-to-all-start.1) | async-done | bytes 98336 | tf_op jit(solution)/shard_map/all_to_all | solution.py:136
  69.4 0.7 select_reduce_fusion.1
  (67 shorter events, 1.7 us)
Async XLA Ops:
  0.6 1.8 %copy-start = (bf16[4,256,1024]{2,1,0:T(8,128)(2,1)S(1)}, bf16[4,256,1024]{2,1,0:T(8,128)(2,1)}, u32[]{:S(2)}) copy-start(bf16[4,256,1024]{2,1,0:T(8,128)(2,1)} %param.11) | copy-start | bytes 6291460
  3.1 11.4 %copy-start.2 = (s32[16,2]{0,1:T(2,128)S(1)}, s32[16,2]{0,1:T(2,128)}, u32[]{:S(2)}) copy-start(s32[16,2]{0,1:T(2,128)} %param.16) | copy-start | bytes 388
  3.2 11.9 %copy-start.1 = (f32[6144]{0:T(1024)S(1)}, f32[6144]{0:T(1024)}, u32[]{:S(2)}) copy-start(f32[6144]{0:T(1024)} %param.14) | copy-start | bytes 73732
  5.6 9.7 %collective-permute-start = (f32[1,4,7,128]{3,1,2,0:T(4,128)S(1)}, f32[1,4,7,128]{3,1,2,0:T(4,128)S(1)}, u32[]{:S(2)}, u32[]{:S(2)}) collective-permute-start(f32[1,4,7,128]{3,1,2,0:T(4,128)S(1)} %bitcast.153), channel_id=1, source_target_pairs={{0,1},{1,0},{2,3},{3,2},{4,5},{5,4},{6,7},{7,6},{8,9},{9,8},{10,11... | collective-permute-start | bytes 43016 | tf_op jit(solution)/shard_map/ppermute | solution.py:91
  8.6 10.3 %collective-permute-start.1 = (f32[1,4,7,128]{3,1,2,0:T(4,128)S(1)}, f32[1,4,7,128]{3,1,2,0:T(4,128)S(1)}, u32[]{:S(2)}, u32[]{:S(2)}) collective-permute-start(f32[1,4,7,128]{3,1,2,0:T(4,128)S(1)} %bitcast.152), channel_id=1, source_target_pairs={{0,2},{1,3},{2,0},{3,1},{4,6},{5,7},{6,4},{7,5},{8,10},{9,11},{10,... | collective-permute-start | bytes 43016 | tf_op jit(solution)/shard_map/ppermute | solution.py:91
  10.2 8.7 %collective-permute-start.2 = (f32[1,4,7,128]{3,1,2,0:T(4,128)S(1)}, f32[1,4,7,128]{3,1,2,0:T(4,128)S(1)}, u32[]{:S(2)}, u32[]{:S(2)}) collective-permute-start(f32[1,4,7,128]{3,1,2,0:T(4,128)S(1)} %bitcast.151), channel_id=1, source_target_pairs={{0,3},{1,2},{2,1},{3,0},{4,7},{5,6},{6,5},{7,4},{8,11},{9,10},{10,... | collective-permute-start | bytes 43016 | tf_op jit(solution)/shard_map/ppermute | solution.py:91
  10.2 8.7 %collective-permute-start.3 = (f32[1,4,7,128]{3,1,2,0:T(4,128)S(1)}, f32[1,4,7,128]{3,1,2,0:T(4,128)S(1)}, u32[]{:S(2)}, u32[]{:S(2)}) collective-permute-start(f32[1,4,7,128]{3,1,2,0:T(4,128)S(1)} %bitcast.150), channel_id=1, source_target_pairs={{0,4},{1,5},{2,6},{3,7},{4,0},{5,1},{6,2},{7,3},{8,12},{9,13},{10,... | collective-permute-start | bytes 43016 | tf_op jit(solution)/shard_map/ppermute | solution.py:91
  13.2 5.7 %collective-permute-start.4 = (f32[1,4,7,128]{3,1,2,0:T(4,128)S(1)}, f32[1,4,7,128]{3,1,2,0:T(4,128)S(1)}, u32[]{:S(2)}, u32[]{:S(2)}) collective-permute-start(f32[1,4,7,128]{3,1,2,0:T(4,128)S(1)} %bitcast.154), channel_id=1, source_target_pairs={{0,5},{1,4},{2,7},{3,6},{4,1},{5,0},{6,3},{7,2},{8,13},{9,12},{10,... | collective-permute-start | bytes 43016 | tf_op jit(solution)/shard_map/ppermute | solution.py:91
  15.2 5.5 %collective-permute-start.5 = (f32[1,4,7,128]{3,1,2,0:T(4,128)S(1)}, f32[1,4,7,128]{3,1,2,0:T(4,128)S(1)}, u32[]{:S(2)}, u32[]{:S(2)}) collective-permute-start(f32[1,4,7,128]{3,1,2,0:T(4,128)S(1)} %bitcast.156), channel_id=1, source_target_pairs={{0,6},{1,7},{2,4},{3,5},{4,2},{5,3},{6,0},{7,1},{8,14},{9,15},{10,... | collective-permute-start | bytes 43016 | tf_op jit(solution)/shard_map/ppermute | solution.py:91
  18.8 6.4 %collective-permute-start.6 = (f32[1,4,7,128]{3,1,2,0:T(4,128)S(1)}, f32[1,4,7,128]{3,1,2,0:T(4,128)S(1)}, u32[]{:S(2)}, u32[]{:S(2)}) collective-permute-start(f32[1,4,7,128]{3,1,2,0:T(4,128)S(1)} %bitcast.155), channel_id=1, source_target_pairs={{0,7},{1,6},{2,5},{3,4},{4,3},{5,2},{6,1},{7,0},{8,15},{9,14},{10,... | collective-permute-start | bytes 43016 | tf_op jit(solution)/shard_map/ppermute | solution.py:91
  27.2 11.1 %all-to-all-start = ((bf16[32,4,768]{2,1,0:T(4,128)(2,1)}), bf16[32,4,768]{2,1,0:T(4,128)(2,1)S(1)}, u32[]{:S(2)}, u32[]{:S(2)}) async-start(bf16[32,4,768]{2,1,0:T(4,128)(2,1)} %broadcast_in_dim.117), calls=%async_computation | async-start | bytes 393216 | tf_op jit(solution)/shard_map/all_to_all | solution.py:105
  29.8 9.4 %copy-start.3 = (bf16[6144,4]{0,1:T(4,128)(2,1)S(1)}, bf16[6144,4]{0,1:T(4,128)(2,1)}, u32[]{:S(2)}) copy-start(bf16[6144,4]{0,1:T(4,128)(2,1)} %param.15) | copy-start | bytes 147460
  58.8 10.5 %all-to-all-start.1 = ((bf16[32,2,768]{2,1,0:T(2,128)(2,1)}), bf16[32,2,768]{2,1,0:T(2,128)(2,1)S(1)}, u32[]{:S(2)}, u32[]{:S(2)}) async-start(bf16[32,2,768]{2,1,0:T(2,128)(2,1)} %copy.112), calls=%async_computation.1 | async-start | bytes 196608 | tf_op jit(solution)/shard_map/all_to_all | solution.py:136
